TPU v7x, 32 devices: a whole 2x2x4 slice. The times are simulated.
32 devices in a mesh: fsdp: 8 (over z, y), rows: 4 (over x, core).
Axes of the slice: x: 2, y: 2, z: 4, core: 2. Of those that a mesh axis runs over, the one named last changes fastest.
Arguments:
- frames: bfloat16 [8, 12, 16, 1536], P('fsdp', 'rows'), may hold values from -6 to 6
- kernel: float32 [7, 7, 1536], replicated, may hold values from -0.875 to 0.875
- kernel_bias: float32 [1536], replicated, may hold values from -3 to 3
- layer_norm_weight: float32 [1536], replicated, may hold values from 0.25 to 1.75
- layer_norm_bias: float32 [1536], replicated, may hold values from -3 to 3
- up_weight: bfloat16 [1536, 6144], P('fsdp', 'rows'), may hold values from -1 to 1, as said below
- up_bias: float32 [6144], P('rows'), may hold values from -3 to 3
- grn_gamma: float32 [6144], P('rows'), may hold values from 0.2 to 1
- grn_beta: float32 [6144], P('rows'), may hold values from -3 to 3
- grad_out: bfloat16 [8, 12, 16, 6144], P('fsdp', None, None, 'rows'), may hold values from -8 to 8, as said below
Outputs:
- activation: bfloat16 [8, 12, 16, 6144], P('fsdp', None, None, 'rows')
- frames_grad: bfloat16 [8, 12, 16, 1536], P('fsdp', 'rows')
- up_weight_grad: float32 [1536, 6144], P('fsdp', 'rows')
- kernel_grad: float32 [7, 7, 1536], replicated
Inputs may be any that keep to these rules, and one draw needn't show every extreme that they name: `up_weight`: entries lie within the bounds. `grad_out`: entries lie within the bounds.
All inputs are finite; a program needn't handle non-finite values.
Results may differ from a plain program's by a relative error of at most 0.014.
Values may be sent and summed in bfloat16 or wider, within the bound.
No kernel may reach another device: no remote copies, remote signals or barrier semaphores. Data moves between devices by JAX's collectives and lax.ppermute only.
A program may use at most 64 MiB of HBM per device.

v0:
```python
import jax
import jax.numpy as jnp
from jax import lax
from jax.sharding import PartitionSpec as P

FF = 6144


def extended(block, sides, width):
    for axis, dim in sides:
        count = lax.axis_size(axis)
        forward = [(i, i + 1) for i in range(count - 1)]
        backward = [(target, source) for source, target in forward]
        low = lax.ppermute(
            lax.slice_in_dim(block, block.shape[dim] - width, None, axis=dim), axis, forward
        )
        high = lax.ppermute(lax.slice_in_dim(block, 0, width, axis=dim), axis, backward)
        block = jnp.concatenate([low, block, high], axis=dim)
    return block


def conv_rows(framed, kern, kbias):
    rows = framed.shape[0] - 6
    cols = framed.shape[1]
    wide = jnp.pad(framed, ((0, 0), (3, 3), (0, 0)))
    total = jnp.zeros((rows, cols, framed.shape[2]), jnp.float32) + kbias
    for i in range(kern.shape[0]):
        for j in range(kern.shape[1]):
            total = total + wide[i : i + rows, j : j + cols].astype(jnp.float32) * kern[i, j]
    return total


def back_conv(grad_pad, kern):
    rows = grad_pad.shape[0] - 6
    cols = grad_pad.shape[1]
    wide = jnp.pad(grad_pad, ((0, 0), (3, 3), (0, 0)))
    total = jnp.zeros((rows, cols, grad_pad.shape[2]), jnp.float32)
    for i in range(kern.shape[0]):
        for j in range(kern.shape[1]):
            total = (
                total
                + wide[6 - i : 6 - i + rows, 6 - j : 6 - j + cols].astype(jnp.float32) * kern[i, j]
            )
    return total


def kern_grad(framed, grad_rows):
    rows = grad_rows.shape[0]
    cols = grad_rows.shape[1]
    wide = jnp.pad(framed, ((0, 0), (3, 3), (0, 0)))
    grad_f = grad_rows.astype(jnp.float32)
    parts = []
    for i in range(7):
        for j in range(7):
            parts.append(
                jnp.sum(wide[i : i + rows, j : j + cols].astype(jnp.float32) * grad_f, axis=(0, 1))
            )
    return jnp.stack(parts).reshape(7, 7, grad_rows.shape[2])


def apply_layer_norm(activation_rows, scale_factor, offset_bias):
    centered_input = activation_rows - jnp.mean(activation_rows, axis=-1, keepdims=True)
    inverse_deviation = lax.rsqrt(
        jnp.mean(centered_input * centered_input, axis=-1, keepdims=True) + 1e-06
    )
    standardized_input = centered_input * inverse_deviation
    return (
        (standardized_input * scale_factor + offset_bias).astype(jnp.bfloat16),
        standardized_input,
        inverse_deviation,
    )


def gelu_grad(value):
    return (
        0.5 * (1.0 + jax.scipy.special.erf(value * 0.7071067811865476))
        + value * jnp.exp(-0.5 * value * value) * 0.3989422804014327
    )


def layer_norm_backward(normed_input_gradient, scale_factor, standardized_input, inverse_deviation):
    scaled_output = normed_input_gradient * scale_factor
    return (
        inverse_deviation
        * (
            scaled_output
            - jnp.mean(scaled_output, axis=-1, keepdims=True)
            - standardized_input
            * jnp.mean(scaled_output * standardized_input, axis=-1, keepdims=True)
        )
    ).astype(jnp.bfloat16)


def body(
    frames,
    kernel,
    kernel_bias,
    layer_norm_weight,
    layer_norm_bias,
    up_weight,
    up_bias,
    grn_gamma,
    grn_beta,
    grad_out,
):
    slab = frames[0]
    chans = slab.shape[2]
    columns = lax.all_gather(up_weight, "fsdp", axis=0, tiled=True)
    padded = extended(slab, (("rows", 0),), 3)
    activation_rows = conv_rows(padded, kernel, kernel_bias)
    normed_output, standardized_input, inverse_deviation = apply_layer_norm(
        activation_rows, layer_norm_weight, layer_norm_bias
    )
    whole = lax.all_gather(normed_output, "rows", axis=0, tiled=True)
    height = whole.shape[0]
    cols = whole.shape[1]
    flat = whole.reshape(-1, chans)
    pre = jnp.dot(flat, columns, preferred_element_type=jnp.float32) + up_bias
    post = jax.nn.gelu(pre, approximate=False)
    norms = jnp.sqrt(jnp.sum(post * post, axis=0) + 1e-06)
    cot_f = grad_out[0].reshape(flat.shape[0], -1).astype(jnp.float32)
    dnorm = grn_gamma * jnp.sum(cot_f * post, axis=0)
    norm_total = lax.psum(jnp.sum(norms), "rows")
    denom = norm_total / FF + 1e-06
    ratio = norms / denom
    output = (grn_gamma * (post * ratio) + grn_beta + post).astype(jnp.bfloat16)
    cross = lax.psum(jnp.sum(dnorm * norms), "rows")
    dnorms = dnorm / denom - cross / (denom * denom) / FF
    dpost = cot_f * (1.0 + grn_gamma * ratio) + post * (dnorms / norms)
    dpre = (dpost * gelu_grad(pre)).astype(jnp.bfloat16)
    w_term = lax.dot_general(
        flat, dpre, (((0,), (0,)), ((), ())), preferred_element_type=jnp.float32
    )
    up_grad = lax.psum_scatter(
        w_term.astype(jnp.bfloat16), "fsdp", scatter_dimension=0, tiled=True
    ).astype(jnp.float32)
    dpre_rows = dpre.reshape(height, cols, -1)
    normed_input_gradient = lax.psum_scatter(
        jnp.einsum("hwf,cf->hwc", dpre_rows, columns, preferred_element_type=jnp.float32).astype(
            jnp.bfloat16
        ),
        "rows",
        scatter_dimension=0,
        tiled=True,
    ).astype(jnp.float32)
    activation_gradient = layer_norm_backward(
        normed_input_gradient, layer_norm_weight, standardized_input, inverse_deviation
    )
    grad_pad = extended(activation_gradient, (("rows", 0),), 3)
    dframe = back_conv(grad_pad, kernel).astype(jnp.bfloat16)
    kernel_local = kern_grad(padded, activation_gradient)
    kernel_total = lax.psum(kernel_local, ("fsdp", "rows"))
    activation = output.reshape(1, height, cols, -1)
    return (activation, dframe.reshape((1,) + dframe.shape), up_grad, kernel_total)


def solution(mesh):
    placed = (
        P("fsdp", "rows", None, None),
        P(),
        P(),
        P(),
        P(),
        P("fsdp", "rows"),
        P("rows"),
        P("rows"),
        P("rows"),
        P("fsdp", None, None, "rows"),
    )
    return jax.shard_map(
        body,
        mesh=mesh,
        in_specs=placed,
        out_specs=(
            P("fsdp", None, None, "rows"),
            P("fsdp", "rows", None, None),
            P("fsdp", "rows"),
            P(),
        ),
        check_vma=False,
    )
```

profile of v0, /device:TPU:1, one launch (start us, length us, event | category | flops | bytes accessed | tf_op | source)
XLA Modules:
  0.0 376.6 jit_solution(9324311914852352310)
XLA Ops:
  8.0 2.0 collective-permute-start.1
  9.9 4.5 %collective-permute-start = (bf16[3,16,1536]{2,1,0:T(8,128)(2,1)}, bf16[3,16,1536]{2,1,0:T(8,128)(2,1)S(1)}, u32[]{:S(2)}, u32[]{:S(2)}) collective-permute-start(bf16[3,16,1536]{2,1,0:T(8,128)(2,1)} %bitcast.25), channel_id=1, source_target_pairs={{0,1},{1,2},{2,3},{4,5},{5,6},{6,7},{8,9},{9,10},{10,11},{12,13},{... | collective-permute-start | bytes 442376 | tf_op jit(solution)/shard_map/ppermute | solution.py:14
  14.4 2.0 slice_reduce_fusion.48
  16.4 1.3 slice_reduce_fusion.46
  17.7 1.8 slice_reduce_fusion.47
  20.0 3.4 fusion.158
  24.9 6.9 %all_gather.6 = bf16[12,16,1536]{2,1,0:T(8,128)(2,1)S(1)} all-gather(bf16[3,16,1536]{2,1,0:T(8,128)(2,1)S(1)} %add_convert_fusion.1), channel_id=1, replica_groups=mesh['fsdp'=8,'rows'=4] {'rows'}, dimensions={0}, use_global_device_ids=true | all-gather | bytes 737280 | tf_op jit(solution)/shard_map/all_gather | solution.py:114
  31.8 59.4 %all-gather.2.cloned.1.call-done = bf16[1536,1536]{1,0:T(8,128)(2,1)} async-done(((bf16[192,1536]{1,0:T(8,128)(2,1)}), bf16[1536,1536]{1,0:T(8,128)(2,1)}) %all-gather.2.cloned.1.call-update) | async-done | bytes 4718608 | tf_op jit(solution)/shard_map/all_gather | solution.py:108
  91.2 7.3 %fusion.9 = (f32[1536]{0:T(1024)S(1)}, f32[1536]{0:T(1024)S(1)}, f32[192,1536]{1,0:T(8,128)}, f32[192,1536]{1,0:T(8,128)}) fusion(bf16[1,12,16,1536]{3,2,1,0:T(8,128)(2,1)S(1)} %copy-done.1, f32[1536]{0:T(1024)S(1)} %copy-done.53, bf16[192,1536]{1,0:T(8,128)(2,1)S(1)} %bitcast.21, bf16[1536,1536]{1,0:T(8,128)(2,1)} %all-gather.2.cloned.1.call-done), kind=kOutput, calls=%fused_computation.65 | convolution fusion | flops 926610432 | bytes 8275968 | tf_op jit(solution)/shard_map/dot_general | solution.py:118
  99.2 7.3 %all-reduce.2 = (f32[]{:T(128)}, f32[]{:T(128)}) all-reduce(f32[]{:T(128)} %get-tuple-element.115, f32[]{:T(128)} %get-tuple-element.114), channel_id=1, replica_groups=mesh['fsdp'=8,'rows'=4] {'rows'}, use_global_device_ids=true, to_apply=%region_4.5 | all-reduce | flops 2 | bytes 16 | tf_op jit(solution)/shard_map/psum | solution.py:123
  107.9 3.2 fusion.8
  111.1 4.8 %fusion.2 = bf16[12,16,1536]{2,1,0:T(8,128)(2,1)} fusion(bf16[12,16,1536]{2,1,0:T(8,128)(2,1)S(1)} %bitcast.23, bf16[1536,1536]{1,0:T(8,128)(2,1)} %all-gather.2.cloned.1.call-done), kind=kOutput, calls=%fused_computation.54 | convolution fusion | flops 906264576 | bytes 5898240 | tf_op jit(solution)/shard_map/hwf,cf->hwc/dot_general | solution.py:139
  116.0 3.6 convolution_convert_fusion
  119.7 16.9 %reduce-scatter.3.cloned.1.call-done = bf16[3,16,1536]{2,1,0:T(8,128)(2,1)} async-done(((bf16[12,16,1536]{2,1,0:T(8,128)(2,1)}), bf16[3,16,1536]{2,1,0:T(8,128)(2,1)}) %reduce-scatter.3.cloned.1.call-update) | async-done | bytes 147472 | tf_op jit(solution)/shard_map/reduce_scatter | solution.py:138
  136.6 1.1 fusion.147
  137.7 1.9 fusion.145
  139.6 2.8 collective-permute-start.3
  142.3 3.0 collective-permute-start.2
  148.1 0.8 reshape.62
  149.3 2.8 fusion.153
  152.1 83.8 %reduce-scatter.5.cloned.1.call-done = bf16[192,1536]{1,0:T(8,128)(2,1)} async-done(((bf16[1536,1536]{1,0:T(8,128)(2,1)}), bf16[192,1536]{1,0:T(8,128)(2,1)}) %reduce-scatter.5.cloned.1.call-update) | async-done | bytes 589840 | tf_op jit(solution)/shard_map/reduce_scatter | solution.py:134
  235.9 2.2 convert_element_type.489
  238.1 130.2 %all-reduce.5.cloned.1.call-done = f32[7,7,1536]{2,1,0:T(8,128)} async-done(((f32[7,7,1536]{2,1,0:T(8,128)}), f32[7,7,1536]{2,1,0:T(8,128)}) %all-reduce.5.cloned.1.call-update) | async-done | bytes 301072 | tf_op jit(solution)/shard_map/psum | solution.py:152
  368.3 1.7 copy.15
  (181 shorter events, 5.7 us)
Async XLA Ops:
  7.2 12.6 %copy-start = (bf16[1,3,16,1536]{3,2,1,0:T(8,128)(2,1)S(1)}, bf16[1,3,16,1536]{3,2,1,0:T(8,128)(2,1)}, u32[]{:S(2)}) copy-start(bf16[1,3,16,1536]{3,2,1,0:T(8,128)(2,1)} %param.10) | copy-start | bytes 442372
  7.2 12.8 %copy-start.52 = (f32[1536]{0:T(1024)S(1)}, f32[1536]{0:T(1024)}, u32[]{:S(2)}) copy-start(f32[1536]{0:T(1024)} %param.12) | copy-start | bytes 18436
  7.2 84.0 %all-gather.2.cloned.1.call-start = ((), (), s32[]{:S(2)}) async-start(), calls=%async_computation.2 | async-start | bytes 5308416 | tf_op jit(solution)/shard_map/all_gather | solution.py:108
  7.9 128.7 %reduce-scatter.3.cloned.1.call-start = ((), (), s32[]{:S(2)}) async-start(), calls=%async_computation.3 | async-start | bytes 737280 | tf_op jit(solution)/shard_map/reduce_scatter | solution.py:138
  8.0 11.7 %collective-permute-start.1 = (bf16[3,16,1536]{2,1,0:T(8,128)(2,1)}, bf16[3,16,1536]{2,1,0:T(8,128)(2,1)S(1)}, u32[]{:S(2)}, u32[]{:S(2)}) collective-permute-start(bf16[3,16,1536]{2,1,0:T(8,128)(2,1)} %bitcast.24), channel_id=1, source_target_pairs={{1,0},{2,1},{3,2},{5,4},{6,5},{7,6},{9,8},{10,9},{11,10},{13,12},{... | collective-permute-start | bytes 442376 | tf_op jit(solution)/shard_map/ppermute | solution.py:17
  9.9 9.8 %collective-permute-start = (bf16[3,16,1536]{2,1,0:T(8,128)(2,1)}, bf16[3,16,1536]{2,1,0:T(8,128)(2,1)S(1)}, u32[]{:S(2)}, u32[]{:S(2)}) collective-permute-start(bf16[3,16,1536]{2,1,0:T(8,128)(2,1)} %bitcast.25), channel_id=1, source_target_pairs={{0,1},{1,2},{2,3},{4,5},{5,6},{6,7},{8,9},{9,10},{10,11},{12,13},{... | collective-permute-start | bytes 442376 | tf_op jit(solution)/shard_map/ppermute | solution.py:14
  17.7 5.7 %copy-start.4 = (f32[1536]{0:T(1024)}, f32[1536]{0:T(1024)S(1)}, u32[]{:S(2)}) copy-start(f32[1536]{0:T(1024)S(1)} %get-tuple-element.99) | copy-start | bytes 18436
  17.7 5.7 %copy-start.6 = (f32[1536]{0:T(1024)}, f32[1536]{0:T(1024)S(1)}, u32[]{:S(2)}) copy-start(f32[1536]{0:T(1024)S(1)} %get-tuple-element.100) | copy-start | bytes 18436
  19.5 3.9 %copy-start.8 = (f32[1536]{0:T(1024)}, f32[1536]{0:T(1024)S(1)}, u32[]{:S(2)}) copy-start(f32[1536]{0:T(1024)S(1)} %get-tuple-element.71) | copy-start | bytes 18436
  19.5 3.9 %copy-start.10 = (f32[1536]{0:T(1024)}, f32[1536]{0:T(1024)S(1)}, u32[]{:S(2)}) copy-start(f32[1536]{0:T(1024)S(1)} %get-tuple-element.72) | copy-start | bytes 18436
  19.5 3.9 %copy-start.12 = (f32[1536]{0:T(1024)}, f32[1536]{0:T(1024)S(1)}, u32[]{:S(2)}) copy-start(f32[1536]{0:T(1024)S(1)} %get-tuple-element.73) | copy-start | bytes 18436
  19.5 3.9 %copy-start.14 = (f32[1536]{0:T(1024)}, f32[1536]{0:T(1024)S(1)}, u32[]{:S(2)}) copy-start(f32[1536]{0:T(1024)S(1)} %get-tuple-element.74) | copy-start | bytes 18436
  20.0 4.8 %copy-start.3 = (f32[1536]{0:T(1024)S(1)}, f32[1536]{0:T(1024)}, u32[]{:S(2)}) copy-start(f32[1536]{0:T(1024)} %param.13) | copy-start | bytes 18436
  20.0 4.8 %copy-start.50 = (f32[1536]{0:T(1024)S(1)}, f32[1536]{0:T(1024)}, u32[]{:S(2)}) copy-start(f32[1536]{0:T(1024)} %param.14) | copy-start | bytes 18436
  23.6 67.6 %copy-start.1 = (bf16[1,12,16,1536]{3,2,1,0:T(8,128)(2,1)S(1)}, bf16[1,12,16,1536]{3,2,1,0:T(8,128)(2,1)}, u32[]{:S(2)}) copy-start(bf16[1,12,16,1536]{3,2,1,0:T(8,128)(2,1)} %param.19) | copy-start | bytes 1769476
  23.6 67.6 %copy-start.53 = (f32[1536]{0:T(1024)S(1)}, f32[1536]{0:T(1024)}, u32[]{:S(2)}) copy-start(f32[1536]{0:T(1024)} %param.16) | copy-start | bytes 18436
  91.2 7.4 %copy-start.2 = (f32[1536]{0:T(1024)S(1)}, f32[1536]{0:T(1024)}, u32[]{:S(2)}) copy-start(f32[1536]{0:T(1024)} %param.17) | copy-start | bytes 18436
  91.2 16.7 %copy-start.51 = (f32[1536]{0:T(1024)S(1)}, f32[1536]{0:T(1024)}, u32[]{:S(2)}) copy-start(f32[1536]{0:T(1024)} %param.18) | copy-start | bytes 18436
  116.0 119.9 %reduce-scatter.5.cloned.1.call-start = ((), (), s32[]{:S(2)}) async-start(), calls=%async_computation.4 | async-start | bytes 5308416 | tf_op jit(solution)/shard_map/reduce_scatter | solution.py:134
  119.6 17.0 %copy-start.47 = (f32[3,16]{1,0:T(4,128)S(1)}, f32[3,16]{1,0:T(4,128)}, u32[]{:S(2)}) copy-start(f32[3,16]{1,0:T(4,128)} %copy-done.46) | copy-start | bytes 580
  119.6 17.0 %copy-start.49 = (f32[3,16]{1,0:T(4,128)S(1)}, f32[3,16]{1,0:T(4,128)}, u32[]{:S(2)}) copy-start(f32[3,16]{1,0:T(4,128)} %copy-done.48) | copy-start | bytes 580
  119.6 248.7 %all-reduce.5.cloned.1.call-start = ((), (), s32[]{:S(2)}) async-start(), calls=%async_computation.5 | async-start | bytes 688128 | tf_op jit(solution)/shard_map/psum | solution.py:152
  139.6 9.3 %collective-permute-start.3 = (bf16[3,16,1536]{2,1,0:T(8,128)(2,1)S(1)}, bf16[3,16,1536]{2,1,0:T(8,128)(2,1)S(1)}, u32[]{:S(2)}, u32[]{:S(2)}) collective-permute-start(bf16[3,16,1536]{2,1,0:T(8,128)(2,1)S(1)} %get-tuple-element.118), channel_id=1, source_target_pairs={{1,0},{2,1},{3,2},{5,4},{6,5},{7,6},{9,8},{10,9},{11,10},{13,12},{... | collective-permute-start | bytes 442376 | tf_op jit(solution)/shard_map/ppermute | solution.py:17
  142.3 6.6 %collective-permute-start.2 = (bf16[3,16,1536]{2,1,0:T(8,128)(2,1)S(1)}, bf16[3,16,1536]{2,1,0:T(8,128)(2,1)S(1)}, u32[]{:S(2)}, u32[]{:S(2)}) collective-permute-start(bf16[3,16,1536]{2,1,0:T(8,128)(2,1)S(1)} %get-tuple-element.118), channel_id=1, source_target_pairs={{0,1},{1,2},{2,3},{4,5},{5,6},{6,7},{8,9},{9,10},{10,11},{12,13},{... | collective-permute-start | bytes 442376 | tf_op jit(solution)/shard_map/ppermute | solution.py:14
  (38 other events, 86.1 us)
Sparse Core Ops, SparseCore 0:
  10.2 80.9 all-gather.1
  116.1 20.4 reduce-scatter.2
  140.3 95.5 reduce-scatter.4
  241.7 126.5 all-reduce.4
where the time goes:
time: 377 us
  waiting for transfers between devices  291 us (77%)
  other arithmetic  17.4 us (5%)
  between operations  16.3 us (4%)
  matrix products  15.7 us (4%)
  blocking collectives  14.2 us (4%)
  starting transfers between devices  12.3 us (3%)
  local copies, waits for them, and re-layouts  9.57 us (3%)
    psum x1, waiting for transfers between devices, body(): kernel_total = lax.psum(kernel_local, ('fsdp', 'rows'))  130 us
    reduce_scatter x1, waiting for transfers between devices, body(): lax.psum_scatter(w_term.astype(jnp.bfloat16), 'fsdp', scatter_dimension=0...  83.8 us
    all_gather x1, waiting for transfers between devices, body(): columns = lax.all_gather(up_weight, 'fsdp', axis=0, tiled=True)  59.4 us
    reduce_scatter x1, waiting for transfers between devices, body(): lax.psum_scatter(jnp.einsum('hwf,cf->hwc', dpre_rows, columns, preferred_...  16.9 us
  transfers between devices with their start and end apart: 8, of which 4 were waited for; matrix products, arithmetic and copies ran while one was open for 6% of the time, Pallas kernels for 0%

commit v1 on v0

--- a/solution.py
+++ b/solution.py
@@ -149,7 +149,7 @@
     grad_pad = extended(activation_gradient, (("rows", 0),), 3)
     dframe = back_conv(grad_pad, kernel).astype(jnp.bfloat16)
     kernel_local = kern_grad(padded, activation_gradient)
-    kernel_total = lax.psum(kernel_local, ("fsdp", "rows"))
+    kernel_total = jnp.sum(lax.all_gather(kernel_local, ("fsdp", "rows")), axis=0)
     activation = output.reshape(1, height, cols, -1)
     return (activation, dframe.reshape((1,) + dframe.shape), up_grad, kernel_total)
 

time: 377 us -> 342 us (0.907)
  waiting for transfers between devices: 291 us -> 251 us
  other arithmetic: 17.4 us -> 23.5 us
    psum x1 -> x0, waiting for transfers between devices: 130 us -> none  [body(): kernel_total = lax.psum(kernel_local, ('fsdp', 'rows'))]
    all_gather x0 -> x1, waiting for transfers between devices: none -> 90.3 us  [body(): lax.all_gather(kernel_local, ('fsdp', 'rows'))]
    reduce_sum x0 -> x1, other arithmetic: none -> 6.18 us  [body(): jnp.sum(lax.all_gather(kernel_local, ('fsdp', 'rows')), axis=0)]
  transfers between devices with their start and end apart: 8 -> 8, of which waited for: 4 -> 6; matrix products, arithmetic and copies ran while one was open for 6% -> 7% of each run, Pallas kernels for 0% -> 0%
where the time goes in v1:
time: 342 us; the launch traced here: 341 us
  waiting for transfers between devices  251 us (73%)
  other arithmetic  23.5 us (7%)
  between operations  16.2 us (5%)
  matrix products  15.8 us (5%)
  blocking collectives  14.2 us (4%)
  starting transfers between devices  12.3 us (4%)
  local copies, waits for them, and re-layouts  7.76 us (2%)
    all_gather x1, waiting for transfers between devices, body(): lax.all_gather(kernel_local, ('fsdp', 'rows'))  90.3 us
    reduce_scatter x1, waiting for transfers between devices, body(): lax.psum_scatter(w_term.astype(jnp.bfloat16), 'fsdp', scatter_dimension=0...  81.5 us
    all_gather x1, waiting for transfers between devices, body(): columns = lax.all_gather(up_weight, 'fsdp', axis=0, tiled=True)  59.5 us
    reduce_scatter x1, waiting for transfers between devices, body(): lax.psum_scatter(jnp.einsum('hwf,cf->hwc', dpre_rows, columns, preferred_...  16.6 us
    ppermute x2, starting transfers between devices, extended(): lax.ppermute(lax.slice_in_dim(block, block.shape[dim] - width, None, axis...  7.45 us
    dot_general x1, matrix products, body(): pre = jnp.dot(flat, columns, preferred_element_type=jnp.float32) + up_bias  7.34 us
    psum x1, blocking collectives, body(): norm_total = lax.psum(jnp.sum(norms), 'rows')  7.3 us
    all_gather x1, blocking collectives, body(): whole = lax.all_gather(normed_output, 'rows', axis=0, tiled=True)  6.86 us
  transfers between devices with their start and end apart: 8, of which 6 were waited for; matrix products, arithmetic and copies ran while one was open for 7% of the time, Pallas kernels for 0%

profile of v1, /device:TPU:1, one launch (start us, length us, event | category | flops | bytes accessed | tf_op | source)
XLA Modules:
  0.0 340.6 jit_solution(8635793611127891942)
XLA Ops:
  8.0 2.0 collective-permute-start.1
  9.9 4.5 %collective-permute-start = (bf16[3,16,1536]{2,1,0:T(8,128)(2,1)}, bf16[3,16,1536]{2,1,0:T(8,128)(2,1)S(1)}, u32[]{:S(2)}, u32[]{:S(2)}) collective-permute-start(bf16[3,16,1536]{2,1,0:T(8,128)(2,1)} %bitcast.25), channel_id=1, source_target_pairs={{0,1},{1,2},{2,3},{4,5},{5,6},{6,7},{8,9},{9,10},{10,11},{12,13},{... | collective-permute-start | bytes 442376 | tf_op jit(solution)/shard_map/ppermute | solution.py:14
  14.4 1.8 slice_reduce_fusion.48
  16.2 1.4 slice_reduce_fusion.46
  17.6 1.8 slice_reduce_fusion.47
  19.9 3.4 %fusion.158 = (f32[3,16]{1,0:T(4,128)S(1)}, f32[3,16,1536]{2,1,0:T(8,128)S(1)}) fusion(f32[1536]{0:T(1024)S(1)} %get-tuple-element.99, bf16[9,22,1536]{2,1,0:T(8,128)(2,1)S(1)} %select_maximum_fusion.2, f32[1536]{0:T(1024)S(1)} %get-tuple-element.100, f32[1536]{0:T(1024)S(1)} %get-tuple-element.53, f32[1536]{0:T(1024)S(1)} %get-tuple-element.54, ...), kind=kLoop, calls=%fused_computation.350 | loop fusion | flops 11206608 | bytes 7237824 | tf_op jit(solution)/shard_map/reduce_sum | solution.py:62
  24.8 6.9 %all_gather.9 = bf16[12,16,1536]{2,1,0:T(8,128)(2,1)S(1)} all-gather(bf16[3,16,1536]{2,1,0:T(8,128)(2,1)S(1)} %add_convert_fusion.1), channel_id=1, replica_groups=mesh['fsdp'=8,'rows'=4] {'rows'}, dimensions={0}, use_global_device_ids=true | all-gather | bytes 737280 | tf_op jit(solution)/shard_map/all_gather | solution.py:114
  31.7 59.5 %all-gather.3.cloned.1.call-done = bf16[1536,1536]{1,0:T(8,128)(2,1)} async-done(((bf16[192,1536]{1,0:T(8,128)(2,1)}), bf16[1536,1536]{1,0:T(8,128)(2,1)}) %all-gather.3.cloned.1.call-update) | async-done | bytes 4718608 | tf_op jit(solution)/shard_map/all_gather | solution.py:108
  91.2 7.3 %fusion.9 = (f32[1536]{0:T(1024)S(1)}, f32[1536]{0:T(1024)S(1)}, f32[192,1536]{1,0:T(8,128)}, f32[192,1536]{1,0:T(8,128)}) fusion(bf16[1,12,16,1536]{3,2,1,0:T(8,128)(2,1)S(1)} %copy-done.1, f32[1536]{0:T(1024)S(1)} %copy-done.53, bf16[192,1536]{1,0:T(8,128)(2,1)S(1)} %bitcast.21, bf16[1536,1536]{1,0:T(8,128)(2,1)} %all-gather.3.cloned.1.call-done), kind=kOutput, calls=%fused_computation.65 | convolution fusion | flops 926610432 | bytes 8275968 | tf_op jit(solution)/shard_map/dot_general | solution.py:118
  99.2 7.3 %all-reduce.2 = (f32[]{:T(128)}, f32[]{:T(128)}) all-reduce(f32[]{:T(128)} %get-tuple-element.115, f32[]{:T(128)} %get-tuple-element.114), channel_id=1, replica_groups=mesh['fsdp'=8,'rows'=4] {'rows'}, use_global_device_ids=true, to_apply=%region_4.5 | all-reduce | flops 2 | bytes 16 | tf_op jit(solution)/shard_map/psum | solution.py:123
  107.8 3.2 fusion.8
  111.0 4.8 %fusion.2 = bf16[12,16,1536]{2,1,0:T(8,128)(2,1)} fusion(bf16[12,16,1536]{2,1,0:T(8,128)(2,1)S(1)} %bitcast.23, bf16[1536,1536]{1,0:T(8,128)(2,1)} %all-gather.3.cloned.1.call-done), kind=kOutput, calls=%fused_computation.54 | convolution fusion | flops 906264576 | bytes 5898240 | tf_op jit(solution)/shard_map/hwf,cf->hwc/dot_general | solution.py:139
  115.9 3.6 %convolution_convert_fusion = bf16[1536,1536]{1,0:T(8,128)(2,1)} fusion(bf16[192,1536]{1,0:T(8,128)(2,1)S(1)} %bitcast.22, bf16[192,1536]{1,0:T(8,128)(2,1)S(1)} %get-tuple-element.124), kind=kOutput, calls=%fused_computation | convolution fusion | flops 908328960 | bytes 5898240 | tf_op jit(solution)/shard_map/dot_general | solution.py:131
  119.8 16.6 %reduce-scatter.3.cloned.1.call-done = bf16[3,16,1536]{2,1,0:T(8,128)(2,1)} async-done(((bf16[12,16,1536]{2,1,0:T(8,128)(2,1)}), bf16[3,16,1536]{2,1,0:T(8,128)(2,1)}) %reduce-scatter.3.cloned.1.call-update) | async-done | bytes 147472 | tf_op jit(solution)/shard_map/reduce_scatter | solution.py:138
  136.4 1.1 fusion.147
  137.6 1.9 fusion.145
  143.0 2.6 collective-permute-start.3
  145.5 3.0 collective-permute-start.2
  149.4 1.2 collective-permute-done.2
  151.1 2.8 fusion.153
  153.8 81.5 %reduce-scatter.5.cloned.1.call-done = bf16[192,1536]{1,0:T(8,128)(2,1)} async-done(((bf16[1536,1536]{1,0:T(8,128)(2,1)}), bf16[192,1536]{1,0:T(8,128)(2,1)}) %reduce-scatter.5.cloned.1.call-update) | async-done | bytes 589840 | tf_op jit(solution)/shard_map/reduce_scatter | solution.py:134
  235.4 2.2 convert_element_type.489
  237.6 90.3 %all-gather.5.cloned.1.call-done = f32[32,7,7,1536]{3,2,1,0:T(8,128)} async-done(((f32[1,7,7,1536]{3,2,1,0:T(8,128)}), f32[32,7,7,1536]{3,2,1,0:T(8,128)}) %all-gather.5.cloned.1.call-update) | async-done | bytes 9633808 | tf_op jit(solution)/shard_map/all_gather | solution.py:152
  327.8 6.2 %reduce_sum.579 = f32[7,7,1536]{2,1,0:T(8,128)} reduce(f32[32,7,7,1536]{3,2,1,0:T(8,128)} %all-gather.5.cloned.1.call-done, f32[]{:T(128)} %constant.37.clone.1), dimensions={0}, to_apply=%region_61.62 | reduce | flops 2333184 | bytes 9934852 | tf_op jit(solution)/shard_map/reduce_sum | solution.py:152
  (181 shorter events, 7.5 us)
Async XLA Ops:
  7.2 12.5 %copy-start = (bf16[1,3,16,1536]{3,2,1,0:T(8,128)(2,1)S(1)}, bf16[1,3,16,1536]{3,2,1,0:T(8,128)(2,1)}, u32[]{:S(2)}) copy-start(bf16[1,3,16,1536]{3,2,1,0:T(8,128)(2,1)} %param.10) | copy-start | bytes 442372
  7.2 12.7 %copy-start.52 = (f32[1536]{0:T(1024)S(1)}, f32[1536]{0:T(1024)}, u32[]{:S(2)}) copy-start(f32[1536]{0:T(1024)} %param.12) | copy-start | bytes 18436
  7.2 84.0 %all-gather.3.cloned.1.call-start = ((), (), s32[]{:S(2)}) async-start(), calls=%async_computation.2 | async-start | bytes 5308416 | tf_op jit(solution)/shard_map/all_gather | solution.py:108
  7.9 128.5 %reduce-scatter.3.cloned.1.call-start = ((), (), s32[]{:S(2)}) async-start(), calls=%async_computation.3 | async-start | bytes 737280 | tf_op jit(solution)/shard_map/reduce_scatter | solution.py:138
  8.0 11.6 %collective-permute-start.1 = (bf16[3,16,1536]{2,1,0:T(8,128)(2,1)}, bf16[3,16,1536]{2,1,0:T(8,128)(2,1)S(1)}, u32[]{:S(2)}, u32[]{:S(2)}) collective-permute-start(bf16[3,16,1536]{2,1,0:T(8,128)(2,1)} %bitcast.24), channel_id=1, source_target_pairs={{1,0},{2,1},{3,2},{5,4},{6,5},{7,6},{9,8},{10,9},{11,10},{13,12},{... | collective-permute-start | bytes 442376 | tf_op jit(solution)/shard_map/ppermute | solution.py:17
  9.9 9.7 %collective-permute-start = (bf16[3,16,1536]{2,1,0:T(8,128)(2,1)}, bf16[3,16,1536]{2,1,0:T(8,128)(2,1)S(1)}, u32[]{:S(2)}, u32[]{:S(2)}) collective-permute-start(bf16[3,16,1536]{2,1,0:T(8,128)(2,1)} %bitcast.25), channel_id=1, source_target_pairs={{0,1},{1,2},{2,3},{4,5},{5,6},{6,7},{8,9},{9,10},{10,11},{12,13},{... | collective-permute-start | bytes 442376 | tf_op jit(solution)/shard_map/ppermute | solution.py:14
  23.5 67.7 %copy-start.1 = (bf16[1,12,16,1536]{3,2,1,0:T(8,128)(2,1)S(1)}, bf16[1,12,16,1536]{3,2,1,0:T(8,128)(2,1)}, u32[]{:S(2)}) copy-start(bf16[1,12,16,1536]{3,2,1,0:T(8,128)(2,1)} %param.19) | copy-start | bytes 1769476
  23.5 67.7 %copy-start.53 = (f32[1536]{0:T(1024)S(1)}, f32[1536]{0:T(1024)}, u32[]{:S(2)}) copy-start(f32[1536]{0:T(1024)} %param.16) | copy-start | bytes 18436
  91.2 16.5 %copy-start.51 = (f32[1536]{0:T(1024)S(1)}, f32[1536]{0:T(1024)}, u32[]{:S(2)}) copy-start(f32[1536]{0:T(1024)} %param.18) | copy-start | bytes 18436
  115.9 119.5 %reduce-scatter.5.cloned.1.call-start = ((), (), s32[]{:S(2)}) async-start(), calls=%async_computation.4 | async-start | bytes 5308416 | tf_op jit(solution)/shard_map/reduce_scatter | solution.py:134
  119.5 16.9 %copy-start.47 = (f32[3,16]{1,0:T(4,128)S(1)}, f32[3,16]{1,0:T(4,128)}, u32[]{:S(2)}) copy-start(f32[3,16]{1,0:T(4,128)} %copy-done.46) | copy-start | bytes 580
  119.5 16.9 %copy-start.49 = (f32[3,16]{1,0:T(4,128)S(1)}, f32[3,16]{1,0:T(4,128)}, u32[]{:S(2)}) copy-start(f32[3,16]{1,0:T(4,128)} %copy-done.48) | copy-start | bytes 580
  119.6 208.3 %all-gather.5.cloned.1.call-start = ((), (), s32[]{:S(2)}) async-start(), calls=%async_computation.5 | async-start | bytes 11354112 | tf_op jit(solution)/shard_map/all_gather | solution.py:152
  142.0 8.9 %copy-start.5 = (f32[1536]{0:T(1024)S(1)}, f32[1536]{0:T(1024)}, u32[]{:S(2)}) copy-start(f32[1536]{0:T(1024)} %copy-done.4) | copy-start | bytes 18436
  142.0 8.9 %copy-start.7 = (f32[1536]{0:T(1024)S(1)}, f32[1536]{0:T(1024)}, u32[]{:S(2)}) copy-start(f32[1536]{0:T(1024)} %copy-done.6) | copy-start | bytes 18436
  142.0 8.9 %copy-start.9 = (f32[1536]{0:T(1024)S(1)}, f32[1536]{0:T(1024)}, u32[]{:S(2)}) copy-start(f32[1536]{0:T(1024)} %copy-done.8) | copy-start | bytes 18436
  142.0 8.9 %copy-start.11 = (f32[1536]{0:T(1024)S(1)}, f32[1536]{0:T(1024)}, u32[]{:S(2)}) copy-start(f32[1536]{0:T(1024)} %copy-done.10) | copy-start | bytes 18436
  142.0 8.9 %copy-start.13 = (f32[1536]{0:T(1024)S(1)}, f32[1536]{0:T(1024)}, u32[]{:S(2)}) copy-start(f32[1536]{0:T(1024)} %copy-done.12) | copy-start | bytes 18436
  142.0 8.9 %copy-start.15 = (f32[1536]{0:T(1024)S(1)}, f32[1536]{0:T(1024)}, u32[]{:S(2)}) copy-start(f32[1536]{0:T(1024)} %copy-done.14) | copy-start | bytes 18436
  142.0 8.9 %copy-start.17 = (f32[1536]{0:T(1024)S(1)}, f32[1536]{0:T(1024)}, u32[]{:S(2)}) copy-start(f32[1536]{0:T(1024)} %copy-done.16) | copy-start | bytes 18436
  142.0 8.9 %copy-start.19 = (f32[1536]{0:T(1024)S(1)}, f32[1536]{0:T(1024)}, u32[]{:S(2)}) copy-start(f32[1536]{0:T(1024)} %copy-done.18) | copy-start | bytes 18436
  142.0 8.9 %copy-start.21 = (f32[1536]{0:T(1024)S(1)}, f32[1536]{0:T(1024)}, u32[]{:S(2)}) copy-start(f32[1536]{0:T(1024)} %copy-done.20) | copy-start | bytes 18436
  143.0 6.5 %collective-permute-start.3 = (bf16[3,16,1536]{2,1,0:T(8,128)(2,1)S(1)}, bf16[3,16,1536]{2,1,0:T(8,128)(2,1)S(1)}, u32[]{:S(2)}, u32[]{:S(2)}) collective-permute-start(bf16[3,16,1536]{2,1,0:T(8,128)(2,1)S(1)} %get-tuple-element.118), channel_id=1, source_target_pairs={{1,0},{2,1},{3,2},{5,4},{6,5},{7,6},{9,8},{10,9},{11,10},{13,12},{... | collective-permute-start | bytes 442376 | tf_op jit(solution)/shard_map/ppermute | solution.py:17
  145.5 5.1 %collective-permute-start.2 = (bf16[3,16,1536]{2,1,0:T(8,128)(2,1)S(1)}, bf16[3,16,1536]{2,1,0:T(8,128)(2,1)S(1)}, u32[]{:S(2)}, u32[]{:S(2)}) collective-permute-start(bf16[3,16,1536]{2,1,0:T(8,128)(2,1)S(1)} %get-tuple-element.118), channel_id=1, source_target_pairs={{0,1},{1,2},{2,3},{4,5},{5,6},{6,7},{8,9},{9,10},{10,11},{12,13},{... | collective-permute-start | bytes 442376 | tf_op jit(solution)/shard_map/ppermute | solution.py:14
  (38 other events, 210.5 us)
Sparse Core Ops, SparseCore 0:
  10.2 80.9 all-gather.2
  116.0 20.4 reduce-scatter.2
  140.1 95.2 reduce-scatter.4
  238.7 89.1 all-gather.4
